TPU v7x, 32 devices: a whole 2x2x4 slice. The times are simulated.
32 devices in a mesh: dp: 4 (over z), fsdp: 2 (over x), rows: 4 (over y, core).
Axes of the slice: x: 2, y: 2, z: 4, core: 2. Of those that a mesh axis runs over, the one named last changes fastest.
Arguments:
- feature_maps: bfloat16 [8, 16, 32, 1536], P(('dp', 'fsdp'), 'rows'), may hold values from -30 to 30
- dw_kernel: float32 [7, 7, 1536], replicated, may hold values from -0.875 to 0.875
- norm_gain: float32 [1536], replicated, may hold values from 0.5 to 1.5
- w_up: bfloat16 [1536, 6144], P(('dp', 'rows'), 'fsdp'), may hold values from -0.15625 to 0.15625
- w_down: bfloat16 [6144, 1536], P('fsdp', ('dp', 'rows')), may hold values from -0.078125 to 0.078125
- layer_scale: float32 [1536], replicated, may hold values from 0.3 to 1.5
- d_out: bfloat16 [8, 16, 32, 1536], P(('dp', 'fsdp'), 'rows'), may hold values from -20 to 20
Outputs:
- result: bfloat16 [8, 16, 32, 1536], P(('dp', 'fsdp'), 'rows')
- grad_x: bfloat16 [8, 16, 32, 1536], P(('dp', 'fsdp'), 'rows')
- grad_up: float32 [1536, 6144], P(('dp', 'rows'), 'fsdp')
- grad_down: float32 [6144, 1536], P('fsdp', ('dp', 'rows'))
- grad_kernel: float32 [7, 7, 1536], replicated
- grad_gain: float32 [1536], replicated
- grad_scale: float32 [1536], replicated
All inputs are finite; a program needn't handle non-finite values.
Results may differ from a plain program's by a relative error of at most 0.0075.
Values may be sent and summed in bfloat16 or wider, within the bound.
No kernel may reach another device: no remote copies, remote signals or barrier semaphores. Data moves between devices by JAX's collectives and lax.ppermute only.
A program may use at most 128 MiB of HBM per device.

v0:
```python
import math
import jax
import jax.numpy as jnp
from jax import lax
from jax.sharding import PartitionSpec as P

KS = 7
norm_eps = 1e-06
inv_root_two = 1.0 / math.sqrt(2.0)
inv_root_two_pi = 1.0 / math.sqrt(2.0 * math.pi)
contract_rows = (((0,), (0,)), ((), ()))
contract_cols = (((1,), (1,)), ((), ()))


def padded_2(x, sides, width):
    for axis, dim in sides:
        devices, length = (lax.axis_size(axis), x.shape[dim])
        up = [(i, (i + 1) % devices) for i in range(devices - 1)]
        down = [(j, i) for i, j in up]
        last = lax.slice_in_dim(x, length - width, length, axis=dim)
        leading = lax.slice_in_dim(x, 0, width, axis=dim)
        before = lax.ppermute(last, axis, up)
        after = lax.ppermute(leading, axis, down)
        x = jnp.concatenate([before, x, after], axis=dim)
    return x


def gelu_exact(values):
    return 0.5 * values * (1.0 + jax.scipy.special.erf(values * inv_root_two))


def gelu_slope(values):
    cdf_part = 0.5 * (1.0 + jax.scipy.special.erf(values * inv_root_two))
    return cdf_part + values * jnp.exp(-0.5 * values * values) * inv_root_two_pi


def small_sums(kernel_part, gain_part, scale_part, width):
    every = ("dp", "fsdp", "rows")
    devices = lax.axis_size(every)
    packed = jnp.concatenate(
        [kernel_part.reshape(KS * KS, width), gain_part[None], scale_part[None]], axis=0
    )
    count = packed.shape[0]
    per = -(-count // devices)
    packed = jnp.pad(packed, ((0, per * devices - count), (0, 0)))
    mine = lax.all_to_all(packed.reshape(devices, per, width), every, 0, 0, tiled=True).sum(0)
    spread = jnp.broadcast_to(mine[None], (devices, per, width))
    total = lax.all_to_all(spread, every, 0, 0, tiled=True).reshape(devices * per, width)
    kernel_sum = total[: KS * KS].reshape(KS, KS, width)
    return (kernel_sum, total[KS * KS], total[KS * KS + 1])


def body(feature_maps, dw_kernel, norm_gain, w_up, w_down, layer_scale, d_out):
    scenes, strip, across, width = feature_maps.shape
    cells = scenes * strip * across
    hid_axes = ("fsdp", "rows")
    dp_size, row_size = (lax.axis_size("dp"), lax.axis_size("rows"))
    block_c, hid_f = w_up.shape
    sub = hid_f // row_size
    pieces = w_up.reshape(block_c, row_size, sub).transpose(1, 0, 2)
    pieces = jnp.broadcast_to(pieces[None], (dp_size, row_size, block_c, sub))
    pieces = pieces.reshape(dp_size * row_size, block_c, sub)
    up_loc = lax.all_to_all(pieces, ("dp", "rows"), 0, 0, tiled=True)
    up_loc = up_loc.reshape(dp_size * row_size * block_c, sub)
    down_loc = lax.all_to_all(w_down, "rows", 0, 1, tiled=True)
    down_loc = lax.all_gather(down_loc, "dp", axis=1, tiled=True)
    cotan = d_out.reshape(cells, width).astype(jnp.float32)
    back = (cotan * layer_scale).astype(jnp.bfloat16)
    rimmed = padded_2(feature_maps, (("rows", 1),), 3)
    padded = jnp.pad(rimmed.astype(jnp.float32), ((0, 0), (0, 0), (3, 3), (0, 0)))
    filtered = jnp.zeros(feature_maps.shape, jnp.float32)
    for row_off in range(KS):
        for col_off in range(KS):
            filtered = (
                filtered
                + padded[:, row_off : row_off + strip, col_off : col_off + across, :]
                * dw_kernel[row_off, col_off]
            )
    flat = filtered.reshape(cells, width)
    average = jnp.mean(flat, axis=-1, keepdims=True)
    center = flat - average
    variance = jnp.mean(center * center, axis=-1, keepdims=True)
    rstd = lax.rsqrt(variance + norm_eps)
    normed = center * rstd
    scaled = (normed * norm_gain).astype(jnp.bfloat16)
    pair = lax.all_gather(jnp.stack([scaled, back]), hid_axes, axis=1, tiled=True)
    gathered, back_all = (pair[0], pair[1])
    hidden = jnp.dot(gathered, up_loc, preferred_element_type=jnp.float32)
    active = gelu_exact(hidden).astype(jnp.bfloat16)
    mlp_terms = jnp.dot(active, down_loc, preferred_element_type=jnp.float32)
    down_part_t = lax.dot_general(
        back_all, active, contract_rows, preferred_element_type=jnp.float32
    )
    slope_in = lax.dot_general(
        back_all, down_loc, contract_cols, preferred_element_type=jnp.float32
    )
    hidden_grad = (slope_in * gelu_slope(hidden)).astype(jnp.bfloat16)
    up_part = lax.dot_general(
        gathered, hidden_grad, contract_rows, preferred_element_type=jnp.float32
    )
    norm_terms = lax.dot_general(
        hidden_grad, up_loc, contract_cols, preferred_element_type=jnp.float32
    )
    sums = lax.psum_scatter(
        jnp.stack([mlp_terms, norm_terms]).astype(jnp.bfloat16),
        hid_axes,
        scatter_dimension=1,
        tiled=True,
    ).astype(jnp.float32)
    branch, norm_grad = (sums[0], sums[1])
    resid = feature_maps.reshape(cells, width).astype(jnp.float32)
    result = (resid + layer_scale * branch).astype(jnp.bfloat16).reshape(feature_maps.shape)
    scale_part = jnp.sum(cotan * branch, axis=0)
    down_blocks = down_part_t.astype(jnp.bfloat16).reshape(dp_size, -1, sub)
    down_sum = lax.all_to_all(down_blocks, "dp", 0, 0, tiled=True).astype(jnp.float32).sum(0)
    up_sum = lax.psum_scatter(up_part.astype(jnp.bfloat16), "dp", scatter_dimension=0, tiled=True)
    grad_sums = jnp.stack([up_sum, down_sum.astype(jnp.bfloat16)])
    gain_part = jnp.sum(norm_grad * normed, axis=0)
    scaled_grad = norm_grad * norm_gain
    conv_grad = rstd * (
        scaled_grad
        - jnp.mean(scaled_grad, axis=-1, keepdims=True)
        - normed * jnp.mean(scaled_grad * normed, axis=-1, keepdims=True)
    )
    conv_grad = conv_grad.reshape(feature_maps.shape)
    grad_rim = padded_2(conv_grad.astype(jnp.bfloat16), (("rows", 1),), 3).astype(conv_grad.dtype)
    grad_pad = jnp.pad(grad_rim, ((0, 0), (0, 0), (3, 3), (0, 0)))
    kernel_rows = []
    back_conv = jnp.zeros(feature_maps.shape, jnp.float32)
    for row_off in range(KS):
        for col_off in range(KS):
            window = padded[:, row_off : row_off + strip, col_off : col_off + across, :]
            kernel_rows.append(jnp.sum(window * conv_grad, axis=(0, 1, 2)))
            back_conv = (
                back_conv
                + grad_pad[
                    :, 6 - row_off : 6 - row_off + strip, 6 - col_off : 6 - col_off + across, :
                ]
                * dw_kernel[row_off, col_off]
            )
    kernel_part = jnp.stack(kernel_rows).reshape(KS, KS, width)
    grad_x = (d_out.astype(jnp.float32) + back_conv).astype(jnp.bfloat16)
    grad_kernel, grad_gain, grad_scale = small_sums(kernel_part, gain_part, scale_part, width)
    grad_sums, grad_x, grad_kernel, grad_gain, grad_scale = lax.optimization_barrier(
        (grad_sums, grad_x, grad_kernel, grad_gain, grad_scale)
    )
    grad_sums = lax.all_to_all(grad_sums, "rows", 1, 2, tiled=True).astype(jnp.float32)
    grad_up, grad_down = (grad_sums[0], grad_sums[1].T)
    return (result, grad_x, grad_up, grad_down, grad_kernel, grad_gain, grad_scale)


def solution(mesh):
    return jax.shard_map(
        body,
        mesh=mesh,
        in_specs=(
            P(("dp", "fsdp"), "rows", None, None),
            P(),
            P(),
            P(("dp", "rows"), "fsdp"),
            P("fsdp", ("dp", "rows")),
            P(),
            P(("dp", "fsdp"), "rows", None, None),
        ),
        out_specs=(
            P(("dp", "fsdp"), "rows", None, None),
            P(("dp", "fsdp"), "rows", None, None),
            P(("dp", "rows"), "fsdp"),
            P("fsdp", ("dp", "rows")),
            P(),
            P(),
            P(),
        ),
        check_vma=False,
    )
```

profile of v0, /device:TPU:0, one launch (start us, length us, event | category | flops | bytes accessed | tf_op | source)
XLA Modules:
  0.0 350.1 jit_solution(6042365886521894993)
XLA Ops:
  7.2 1.1 fusion.114
  8.3 2.4 collective-permute-start
  10.7 1.3 collective-permute-start.1
  12.0 1.4 slice_reduce_fusion.48
  13.5 1.8 slice_reduce_fusion.50
  15.4 2.5 slice_reduce_fusion.49
  18.0 1.1 maximum_convert_fusion
  19.2 9.4 %fusion.110 = (f32[4,32]{1,0:T(4,128)S(1)}, f32[1,4,32,1536]{3,2,1,0:T(8,128)S(1)}) fusion(f32[1536]{0:T(1024)S(1)} %get-tuple-element.119, f32[1536]{0:T(1024)S(1)} %get-tuple-element.120, f32[1536]{0:T(1024)S(1)} %get-tuple-element.73, f32[1536]{0:T(1024)S(1)} %get-tuple-element.74, f32[1,10,32,1536]{3,2,1,0:T(8,128)S(1)} %maximum_convert_fusion, ...), kind=kLoop, calls=%fused_computation.332 | loop fusion | flops 19267456 | bytes 8641024 | tf_op jit(solution)/shard_map/reduce_sum | solution.py:80
  29.8 0.9 pad_maximum_fusion.2
  31.0 0.9 copy.45
  31.9 6.1 %all-to-all-start.1 = ((bf16[4,768,96]{1,2,0:T(8,128)(2,1)}), bf16[4,768,96]{1,2,0:T(8,128)(2,1)S(1)}, u32[]{:S(2)}, u32[]{:S(2)}) async-start(bf16[4,768,96]{1,2,0:T(8,128)(2,1)} %bitcast.94), calls=%async_computation.1 | async-start | bytes 1179648 | tf_op jit(solution)/shard_map/all_to_all | solution.py:65
  38.0 2.5 reshape.558
  40.5 2.0 copy.34
  42.5 7.0 %all-to-all-done.1 = bf16[4,768,96]{1,2,0:T(8,128)(2,1)S(1)} async-done(((bf16[4,768,96]{1,2,0:T(8,128)(2,1)}), bf16[4,768,96]{1,2,0:T(8,128)(2,1)S(1)}, u32[]{:S(2)}, u32[]{:S(2)}) %all-to-all-start.1) | async-done | bytes 589856 | tf_op jit(solution)/shard_map/all_to_all | solution.py:65
  49.5 2.9 broadcast_in_dim.8
  52.4 5.3 %all-to-all-start = ((bf16[16,96,768]{2,1,0:T(8,128)(2,1)}), bf16[16,96,768]{2,1,0:T(8,128)(2,1)}, u32[]{:S(2)}, u32[]{:S(2)}) async-start(bf16[16,96,768]{2,1,0:T(8,128)(2,1)} %bitcast.86), calls=%async_computation | async-start | bytes 4718592 | tf_op jit(solution)/shard_map/all_to_all | solution.py:63
  57.8 0.7 all-gather.5.cloned.1.call-update
  58.8 44.8 %all-to-all-done = bf16[16,96,768]{2,1,0:T(8,128)(2,1)} async-done(((bf16[16,96,768]{2,1,0:T(8,128)(2,1)}), bf16[16,96,768]{2,1,0:T(8,128)(2,1)}, u32[]{:S(2)}, u32[]{:S(2)}) %all-to-all-start) | async-done | bytes 2359328 | tf_op jit(solution)/shard_map/all_to_all | solution.py:63
  103.6 7.5 %multiply_convert_fusion = (bf16[1024,768]{1,0:T(8,128)(2,1)}, f32[1024,768]{1,0:T(8,128)}) fusion(bf16[1536,768]{1,0:T(8,128)(2,1)} %bitcast.5, bf16[2,1024,1536]{2,1,0:T(8,128)(2,1)} %all-gather.3.cloned.1.call-done), kind=kOutput, calls=%fused_computation.100 | convolution fusion | flops 2419851264 | bytes 10223616 | tf_op jit(solution)/shard_map/dot_general | solution.py:88
  111.1 43.2 %all-gather.5.cloned.1.call-done = bf16[768,1536]{0,1:T(8,128)(2,1)} async-done(((bf16[768,384]{0,1:T(8,128)(2,1)}), bf16[768,1536]{0,1:T(8,128)(2,1)}) %all-gather.5.cloned.1.call-update) | async-done | bytes 2359312 | tf_op jit(solution)/shard_map/all_gather | solution.py:66
  154.3 6.6 %fusion.7 = bf16[1024,768]{1,0:T(8,128)(2,1)S(1)} fusion(f32[1024,768]{1,0:T(8,128)} %get-tuple-element.134, bf16[768,1536]{0,1:T(8,128)(2,1)} %all-gather.5.cloned.1.call-done, bf16[2,1024,1536]{2,1,0:T(8,128)(2,1)} %all-gather.3.cloned.1.call-done), kind=kOutput, calls=%fused_computation.97 | convolution fusion | flops 2423783424 | bytes 10223616 | tf_op jit(solution)/shard_map/dot_general | solution.py:94
  161.0 5.1 %fusion.1 = bf16[1,1024,1536]{2,1,0:T(8,128)(2,1)S(1)} fusion(bf16[1024,768]{1,0:T(8,128)(2,1)S(1)} %fusion.7, bf16[1536,768]{1,0:T(8,128)(2,1)} %bitcast.5), kind=kOutput, calls=%fused_computation.91 | convolution fusion | flops 2417491968 | bytes 7077888 | tf_op jit(solution)/shard_map/dot_general | solution.py:101
  166.1 2.9 fusion
  169.1 3.2 pad_maximum_fusion
  172.8 6.5 %convolution_convert_fusion.3 = bf16[1536,768]{1,0:T(8,128)(2,1)} fusion(bf16[1024,768]{1,0:T(8,128)(2,1)} %copy-done.61, bf16[2,1024,1536]{2,1,0:T(8,128)(2,1)} %all-gather.3.cloned.1.call-done), kind=kOutput, calls=%fused_computation.89 | convolution fusion | flops 2417098752 | bytes 7077888 | tf_op jit(solution)/shard_map/dot_general | solution.py:98
  179.3 7.1 %convolution_convert_fusion.2 = bf16[1536,768]{1,0:T(8,128)(2,1)} fusion(bf16[1024,768]{1,0:T(8,128)(2,1)} %get-tuple-element.133, bf16[2,1024,1536]{2,1,0:T(8,128)(2,1)} %all-gather.3.cloned.1.call-done), kind=kOutput, calls=%fused_computation.88 | convolution fusion | flops 2417098752 | bytes 7077888 | tf_op jit(solution)/shard_map/dot_general | solution.py:91
  186.4 4.5 %all-to-all-start.2 = ((bf16[4,384,768]{2,1,0:T(8,128)(2,1)}), bf16[4,384,768]{2,1,0:T(8,128)(2,1)}, u32[]{:S(2)}, u32[]{:S(2)}) async-start(bf16[4,384,768]{2,1,0:T(8,128)(2,1)} %bitcast.92), calls=%async_computation.4 | async-start | bytes 4718592 | tf_op jit(solution)/shard_map/all_to_all | solution.py:115
  190.9 42.1 %reduce-scatter.3.cloned.1.call-done = bf16[2,128,1536]{2,1,0:T(8,128)(2,1)} async-done(((bf16[2,1024,1536]{2,1,0:T(8,128)(2,1)}), bf16[2,128,1536]{2,1,0:T(8,128)(2,1)}) %reduce-scatter.3.cloned.1.call-update) | async-done | bytes 786448 | tf_op jit(solution)/shard_map/reduce_scatter | solution.py:104
  233.0 1.4 convert_element_type.120
  234.4 2.1 fusion.104
  237.6 1.3 div.22
  238.9 1.2 broadcast_multiply_fusion.1
  240.1 1.3 div.24
  241.4 1.3 broadcast_in_dim.10
  242.7 1.0 fusion.112
  243.7 2.4 multiply_reduce_fusion
  246.3 2.0 multiply_reduce_fusion.18
  248.4 1.4 multiply_reduce_fusion.36
  250.8 1.0 reshape.563
  251.8 4.7 %all-to-all-start.3 = ((f32[32,2,1536]{2,1,0:T(2,128)}), f32[32,2,1536]{2,1,0:T(2,128)}, u32[]{:S(2)}, u32[]{:S(2)}) async-start(f32[32,2,1536]{2,1,0:T(2,128)} %reshape.563), calls=%async_computation.5 | async-start | bytes 786432 | tf_op jit(solution)/shard_map/all_to_all | solution.py:46
  256.6 2.1 collective-permute-start.2
  258.7 1.5 collective-permute-start.3
  260.2 2.3 reduce_sum.518
  262.5 27.8 %reduce-scatter.5.cloned.1.call-done = bf16[384,768]{1,0:T(8,128)(2,1)} async-done(((bf16[1536,768]{1,0:T(8,128)(2,1)}), bf16[384,768]{1,0:T(8,128)(2,1)}) %reduce-scatter.5.cloned.1.call-update) | async-done | bytes 589840 | tf_op jit(solution)/shard_map/reduce_scatter | solution.py:116
  290.2 1.2 pad_maximum_fusion.1
  291.5 0.7 copy-done.5
  292.2 1.2 maximum_convert_fusion.1
  293.4 1.1 reduce_sum.572
  294.5 0.8 broadcast_in_dim.11
  295.3 4.9 %all-to-all-start.4 = ((f32[32,2,1536]{2,1,0:T(2,128)}), f32[32,2,1536]{2,1,0:T(2,128)S(1)}, u32[]{:S(2)}, u32[]{:S(2)}) async-start(f32[32,2,1536]{2,1,0:T(2,128)} %broadcast_in_dim.11), calls=%async_computation.6 | async-start | bytes 786432 | tf_op jit(solution)/shard_map/all_to_all | solution.py:48
  300.3 8.3 %fusion.97 = bf16[1,4,32,1536]{3,2,1,0:T(8,128)(2,1)} fusion(f32[1,10,32,1536]{3,2,1,0:T(8,128)S(1)} %maximum_convert_fusion.1, f32[1536]{0:T(1024)} %copy-done.16, f32[1536]{0:T(1024)} %copy-done.17, f32[1536]{0:T(1024)} %copy-done.19, f32[1536]{0:T(1024)} %copy-done.20, f32[1536]{0:T(1024)} %copy-done.21, f32[1536]{0:T(1024)} %copy-done.22, ...), kind=kLoop, calls=%fused_computation.195 | loop fusion | flops 19660800 | bytes 8562688 | tf_op jit(solution)/shard_map/convert_element_type | solution.py:142
  308.6 4.8 %all-to-all-done.4 = f32[32,2,1536]{2,1,0:T(2,128)S(1)} async-done(((f32[32,2,1536]{2,1,0:T(2,128)}), f32[32,2,1536]{2,1,0:T(2,128)S(1)}, u32[]{:S(2)}, u32[]{:S(2)}) %all-to-all-start.4) | async-done | bytes 393248 | tf_op jit(solution)/shard_map/all_to_all | solution.py:48
  313.8 0.6 slice_reduce_fusion
  314.4 0.8 reshape.565
  315.2 2.2 copy.37
  317.4 3.5 %all-to-all-start.5 = ((bf16[2,384,768]{2,0,1:T(2,128)(2,1)}), bf16[2,384,768]{2,0,1:T(2,128)(2,1)S(1)}, u32[]{:S(2)}, u32[]{:S(2)}) async-start(bf16[2,384,768]{2,0,1:T(2,128)(2,1)} %copy.37), calls=%async_computation.7 | async-start | bytes 2359296 | tf_op jit(solution)/shard_map/all_to_all | solution.py:147
  321.0 2.0 add_convert_fusion
  322.9 13.8 %all-to-all-done.5 = bf16[2,384,768]{2,0,1:T(2,128)(2,1)S(1)} async-done(((bf16[2,384,768]{2,0,1:T(2,128)(2,1)}), bf16[2,384,768]{2,0,1:T(2,128)(2,1)S(1)}, u32[]{:S(2)}, u32[]{:S(2)}) %all-to-all-start.5) | async-done | bytes 1179680 | tf_op jit(solution)/shard_map/all_to_all | solution.py:147
  336.8 0.8 convert_bitcast_fusion
  337.6 1.8 fusion.111
  339.4 0.8 copy.39
  340.2 1.2 copy.43
  341.4 0.8 copy.38
  342.2 1.2 copy.42
  (199 shorter events, 4.4 us)
Async XLA Ops:
  7.2 96.4 %all-gather.3.cloned.1.call-start = ((), (), s32[]{:S(2)}) async-start(), calls=%async_computation.8 | async-start | bytes 7077888 | tf_op jit(solution)/shard_map/all_gather | solution.py:86
  8.3 9.7 %collective-permute-start = (bf16[1,3,32,1536]{3,2,1,0:T(8,128)(2,1)S(1)}, bf16[1,3,32,1536]{3,2,1,0:T(8,128)(2,1)S(1)}, u32[]{:S(2)}, u32[]{:S(2)}) collective-permute-start(bf16[1,3,32,1536]{3,2,1,0:T(8,128)(2,1)S(1)} %get-tuple-element.131), channel_id=1, source_target_pairs={{0,1},{1,2},{2,3},{4,5},{5,6},{6,7},{8,9},{9,10},{10,11},{12,13},{... | collective-permute-start | bytes 884744 | tf_op jit(solution)/shard_map/ppermute | solution.py:22
  10.7 7.3 %collective-permute-start.1 = (bf16[1,3,32,1536]{3,2,1,0:T(8,128)(2,1)S(1)}, bf16[1,3,32,1536]{3,2,1,0:T(8,128)(2,1)S(1)}, u32[]{:S(2)}, u32[]{:S(2)}) collective-permute-start(bf16[1,3,32,1536]{3,2,1,0:T(8,128)(2,1)S(1)} %get-tuple-element.132), channel_id=1, source_target_pairs={{1,0},{2,1},{3,2},{5,4},{6,5},{7,6},{9,8},{10,9},{11,10},{13,12},{... | collective-permute-start | bytes 884744 | tf_op jit(solution)/shard_map/ppermute | solution.py:23
  13.4 15.3 %copy-start.7 = (f32[1536]{0:T(1024)}, f32[1536]{0:T(1024)S(1)}, u32[]{:S(2)}) copy-start(f32[1536]{0:T(1024)S(1)} %get-tuple-element.111) | copy-start | bytes 18436
  13.4 15.3 %copy-start.9 = (f32[1536]{0:T(1024)}, f32[1536]{0:T(1024)S(1)}, u32[]{:S(2)}) copy-start(f32[1536]{0:T(1024)S(1)} %get-tuple-element.112) | copy-start | bytes 18436
  13.4 15.3 %copy-start.10 = (f32[1536]{0:T(1024)}, f32[1536]{0:T(1024)S(1)}, u32[]{:S(2)}) copy-start(f32[1536]{0:T(1024)S(1)} %get-tuple-element.113) | copy-start | bytes 18436
  13.4 15.3 %copy-start.11 = (f32[1536]{0:T(1024)}, f32[1536]{0:T(1024)S(1)}, u32[]{:S(2)}) copy-start(f32[1536]{0:T(1024)S(1)} %get-tuple-element.114) | copy-start | bytes 18436
  13.4 15.3 %copy-start.12 = (f32[1536]{0:T(1024)}, f32[1536]{0:T(1024)S(1)}, u32[]{:S(2)}) copy-start(f32[1536]{0:T(1024)S(1)} %get-tuple-element.115) | copy-start | bytes 18436
  13.4 15.3 %copy-start.13 = (f32[1536]{0:T(1024)}, f32[1536]{0:T(1024)S(1)}, u32[]{:S(2)}) copy-start(f32[1536]{0:T(1024)S(1)} %get-tuple-element.116) | copy-start | bytes 18436
  13.4 15.3 %copy-start.14 = (f32[1536]{0:T(1024)}, f32[1536]{0:T(1024)S(1)}, u32[]{:S(2)}) copy-start(f32[1536]{0:T(1024)S(1)} %get-tuple-element.117) | copy-start | bytes 18436
  13.4 15.3 %copy-start.15 = (f32[1536]{0:T(1024)}, f32[1536]{0:T(1024)S(1)}, u32[]{:S(2)}) copy-start(f32[1536]{0:T(1024)S(1)} %get-tuple-element.118) | copy-start | bytes 18436
  13.5 15.3 %copy-start.16 = (f32[1536]{0:T(1024)}, f32[1536]{0:T(1024)S(1)}, u32[]{:S(2)}) copy-start(f32[1536]{0:T(1024)S(1)} %get-tuple-element.119) | copy-start | bytes 18436
  13.5 15.3 %copy-start.17 = (f32[1536]{0:T(1024)}, f32[1536]{0:T(1024)S(1)}, u32[]{:S(2)}) copy-start(f32[1536]{0:T(1024)S(1)} %get-tuple-element.120) | copy-start | bytes 18436
  15.2 13.5 %copy-start.18 = (f32[1536]{0:T(1024)}, f32[1536]{0:T(1024)S(1)}, u32[]{:S(2)}) copy-start(f32[1536]{0:T(1024)S(1)} %get-tuple-element.72) | copy-start | bytes 18436
  15.3 13.5 %copy-start.19 = (f32[1536]{0:T(1024)}, f32[1536]{0:T(1024)S(1)}, u32[]{:S(2)}) copy-start(f32[1536]{0:T(1024)S(1)} %get-tuple-element.73) | copy-start | bytes 18436
  15.3 13.5 %copy-start.20 = (f32[1536]{0:T(1024)}, f32[1536]{0:T(1024)S(1)}, u32[]{:S(2)}) copy-start(f32[1536]{0:T(1024)S(1)} %get-tuple-element.74) | copy-start | bytes 18436
  15.3 13.5 %copy-start.21 = (f32[1536]{0:T(1024)}, f32[1536]{0:T(1024)S(1)}, u32[]{:S(2)}) copy-start(f32[1536]{0:T(1024)S(1)} %get-tuple-element.75) | copy-start | bytes 18436
  15.3 13.5 %copy-start.22 = (f32[1536]{0:T(1024)}, f32[1536]{0:T(1024)S(1)}, u32[]{:S(2)}) copy-start(f32[1536]{0:T(1024)S(1)} %get-tuple-element.76) | copy-start | bytes 18436
  15.3 13.5 %copy-start.23 = (f32[1536]{0:T(1024)}, f32[1536]{0:T(1024)S(1)}, u32[]{:S(2)}) copy-start(f32[1536]{0:T(1024)S(1)} %get-tuple-element.77) | copy-start | bytes 18436
  15.3 13.5 %copy-start.24 = (f32[1536]{0:T(1024)}, f32[1536]{0:T(1024)S(1)}, u32[]{:S(2)}) copy-start(f32[1536]{0:T(1024)S(1)} %get-tuple-element.78) | copy-start | bytes 18436
  15.3 13.5 %copy-start.25 = (f32[1536]{0:T(1024)}, f32[1536]{0:T(1024)S(1)}, u32[]{:S(2)}) copy-start(f32[1536]{0:T(1024)S(1)} %get-tuple-element.79) | copy-start | bytes 18436
  15.3 13.5 %copy-start.26 = (f32[1536]{0:T(1024)}, f32[1536]{0:T(1024)S(1)}, u32[]{:S(2)}) copy-start(f32[1536]{0:T(1024)S(1)} %get-tuple-element.80) | copy-start | bytes 18436
  15.3 13.5 %copy-start.27 = (f32[1536]{0:T(1024)}, f32[1536]{0:T(1024)S(1)}, u32[]{:S(2)}) copy-start(f32[1536]{0:T(1024)S(1)} %get-tuple-element.81) | copy-start | bytes 18436
  15.3 13.5 %copy-start.28 = (f32[1536]{0:T(1024)}, f32[1536]{0:T(1024)S(1)}, u32[]{:S(2)}) copy-start(f32[1536]{0:T(1024)S(1)} %get-tuple-element.82) | copy-start | bytes 18436
  15.4 13.5 %copy-start.29 = (f32[1536]{0:T(1024)}, f32[1536]{0:T(1024)S(1)}, u32[]{:S(2)}) copy-start(f32[1536]{0:T(1024)S(1)} %get-tuple-element.83) | copy-start | bytes 18436
  15.4 13.5 %copy-start.30 = (f32[1536]{0:T(1024)}, f32[1536]{0:T(1024)S(1)}, u32[]{:S(2)}) copy-start(f32[1536]{0:T(1024)S(1)} %get-tuple-element.84) | copy-start | bytes 18436
  15.4 13.5 %copy-start.31 = (f32[1536]{0:T(1024)}, f32[1536]{0:T(1024)S(1)}, u32[]{:S(2)}) copy-start(f32[1536]{0:T(1024)S(1)} %get-tuple-element.85) | copy-start | bytes 18436
  15.4 13.5 %copy-start.32 = (f32[1536]{0:T(1024)}, f32[1536]{0:T(1024)S(1)}, u32[]{:S(2)}) copy-start(f32[1536]{0:T(1024)S(1)} %get-tuple-element.86) | copy-start | bytes 18436
  15.4 13.5 %copy-start.33 = (f32[1536]{0:T(1024)}, f32[1536]{0:T(1024)S(1)}, u32[]{:S(2)}) copy-start(f32[1536]{0:T(1024)S(1)} %get-tuple-element.87) | copy-start | bytes 18436
  15.4 13.5 %copy-start.34 = (f32[1536]{0:T(1024)}, f32[1536]{0:T(1024)S(1)}, u32[]{:S(2)}) copy-start(f32[1536]{0:T(1024)S(1)} %get-tuple-element.88) | copy-start | bytes 18436
  15.4 13.5 %copy-start.35 = (f32[1536]{0:T(1024)}, f32[1536]{0:T(1024)S(1)}, u32[]{:S(2)}) copy-start(f32[1536]{0:T(1024)S(1)} %get-tuple-element.89) | copy-start | bytes 18436
  15.4 13.5 %copy-start.36 = (f32[1536]{0:T(1024)}, f32[1536]{0:T(1024)S(1)}, u32[]{:S(2)}) copy-start(f32[1536]{0:T(1024)S(1)} %get-tuple-element.90) | copy-start | bytes 18436
  17.9 11.0 %copy-start.37 = (f32[1536]{0:T(1024)}, f32[1536]{0:T(1024)S(1)}, u32[]{:S(2)}) copy-start(f32[1536]{0:T(1024)S(1)} %get-tuple-element.91) | copy-start | bytes 18436
  17.9 11.0 %copy-start.38 = (f32[1536]{0:T(1024)}, f32[1536]{0:T(1024)S(1)}, u32[]{:S(2)}) copy-start(f32[1536]{0:T(1024)S(1)} %get-tuple-element.92) | copy-start | bytes 18436
  17.9 11.0 %copy-start.39 = (f32[1536]{0:T(1024)}, f32[1536]{0:T(1024)S(1)}, u32[]{:S(2)}) copy-start(f32[1536]{0:T(1024)S(1)} %get-tuple-element.93) | copy-start | bytes 18436
  17.9 11.0 %copy-start.40 = (f32[1536]{0:T(1024)}, f32[1536]{0:T(1024)S(1)}, u32[]{:S(2)}) copy-start(f32[1536]{0:T(1024)S(1)} %get-tuple-element.94) | copy-start | bytes 18436
  18.0 11.0 %copy-start.41 = (f32[1536]{0:T(1024)}, f32[1536]{0:T(1024)S(1)}, u32[]{:S(2)}) copy-start(f32[1536]{0:T(1024)S(1)} %get-tuple-element.95) | copy-start | bytes 18436
  18.0 11.0 %copy-start.42 = (f32[1536]{0:T(1024)}, f32[1536]{0:T(1024)S(1)}, u32[]{:S(2)}) copy-start(f32[1536]{0:T(1024)S(1)} %get-tuple-element.96) | copy-start | bytes 18436
  18.0 11.0 %copy-start.43 = (f32[1536]{0:T(1024)}, f32[1536]{0:T(1024)S(1)}, u32[]{:S(2)}) copy-start(f32[1536]{0:T(1024)S(1)} %get-tuple-element.97) | copy-start | bytes 18436
  18.0 11.0 %copy-start.44 = (f32[1536]{0:T(1024)}, f32[1536]{0:T(1024)S(1)}, u32[]{:S(2)}) copy-start(f32[1536]{0:T(1024)S(1)} %get-tuple-element.98) | copy-start | bytes 18436
  18.0 11.0 %copy-start.45 = (f32[1536]{0:T(1024)}, f32[1536]{0:T(1024)S(1)}, u32[]{:S(2)}) copy-start(f32[1536]{0:T(1024)S(1)} %get-tuple-element.99) | copy-start | bytes 18436
  18.0 11.0 %copy-start.46 = (f32[1536]{0:T(1024)}, f32[1536]{0:T(1024)S(1)}, u32[]{:S(2)}) copy-start(f32[1536]{0:T(1024)S(1)} %get-tuple-element.100) | copy-start | bytes 18436
  19.2 10.3 %copy-start.2 = (bf16[1,4,32,1536]{3,2,1,0:T(8,128)(2,1)S(1)}, bf16[1,4,32,1536]{3,2,1,0:T(8,128)(2,1)}, u32[]{:S(2)}) copy-start(bf16[1,4,32,1536]{3,2,1,0:T(8,128)(2,1)} %param.13) | copy-start | bytes 1179652
  19.2 10.3 %copy-start.6 = (f32[1536]{0:T(1024)S(1)}, f32[1536]{0:T(1024)}, u32[]{:S(2)}) copy-start(f32[1536]{0:T(1024)} %param.9) | copy-start | bytes 18436
  19.2 10.3 %copy-start.47 = (f32[1536]{0:T(1024)S(1)}, f32[1536]{0:T(1024)}, u32[]{:S(2)}) copy-start(f32[1536]{0:T(1024)} %param.12) | copy-start | bytes 18436
  31.9 17.6 %all-to-all-start.1 = ((bf16[4,768,96]{1,2,0:T(8,128)(2,1)}), bf16[4,768,96]{1,2,0:T(8,128)(2,1)S(1)}, u32[]{:S(2)}, u32[]{:S(2)}) async-start(bf16[4,768,96]{1,2,0:T(8,128)(2,1)} %bitcast.94), calls=%async_computation.1 | async-start | bytes 1179648 | tf_op jit(solution)/shard_map/all_to_all | solution.py:65
  49.5 2.9 copy-start.3
  52.4 51.2 %all-to-all-start = ((bf16[16,96,768]{2,1,0:T(8,128)(2,1)}), bf16[16,96,768]{2,1,0:T(8,128)(2,1)}, u32[]{:S(2)}, u32[]{:S(2)}) async-start(bf16[16,96,768]{2,1,0:T(8,128)(2,1)} %bitcast.86), calls=%async_computation | async-start | bytes 4718592 | tf_op jit(solution)/shard_map/all_to_all | solution.py:63
  57.7 96.6 %all-gather.5.cloned.1.call-start = ((), (), s32[]{:S(2)}) async-start(), calls=%async_computation.9 | async-start | bytes 2949120 | tf_op jit(solution)/shard_map/all_gather | solution.py:66
  58.5 174.5 %reduce-scatter.3.cloned.1.call-start = ((), (), s32[]{:S(2)}) async-start(), calls=%async_computation.10 | async-start | bytes 7077888 | tf_op jit(solution)/shard_map/reduce_scatter | solution.py:104
  160.9 5.2 %copy-start.61 = (bf16[1024,768]{1,0:T(8,128)(2,1)}, bf16[1024,768]{1,0:T(8,128)(2,1)S(1)}, u32[]{:S(2)}) copy-start(bf16[1024,768]{1,0:T(8,128)(2,1)S(1)} %fusion.7) | copy-start | bytes 4718596
  161.0 5.2 %copy-start.59 = (bf16[768,1536]{0,1:T(8,128)(2,1)S(1)}, bf16[768,1536]{0,1:T(8,128)(2,1)}, u32[]{:S(2)}) copy-start(bf16[768,1536]{0,1:T(8,128)(2,1)} %all-gather.5.cloned.1.call-done) | copy-start | bytes 7077892
  161.0 5.2 %copy-start.60 = (bf16[1024,768]{1,0:T(8,128)(2,1)S(1)}, bf16[1024,768]{1,0:T(8,128)(2,1)}, u32[]{:S(2)}) copy-start(bf16[1024,768]{1,0:T(8,128)(2,1)} %get-tuple-element.133) | copy-start | bytes 4718596
  172.3 118.0 %reduce-scatter.5.cloned.1.call-start = ((), (), s32[]{:S(2)}) async-start(), calls=%async_computation.11 | async-start | bytes 2949120 | tf_op jit(solution)/shard_map/reduce_scatter | solution.py:116
  186.4 65.4 %all-to-all-start.2 = ((bf16[4,384,768]{2,1,0:T(8,128)(2,1)}), bf16[4,384,768]{2,1,0:T(8,128)(2,1)}, u32[]{:S(2)}, u32[]{:S(2)}) async-start(bf16[4,384,768]{2,1,0:T(8,128)(2,1)} %bitcast.92), calls=%async_computation.4 | async-start | bytes 4718592 | tf_op jit(solution)/shard_map/all_to_all | solution.py:115
  233.0 9.7 %copy-start = (bf16[2,128,1536]{2,1,0:T(8,128)(2,1)S(1)}, bf16[2,128,1536]{2,1,0:T(8,128)(2,1)}, u32[]{:S(2)}) copy-start(bf16[2,128,1536]{2,1,0:T(8,128)(2,1)} %reduce-scatter.3.cloned.1.call-done) | copy-start | bytes 2359300
  251.8 41.5 %all-to-all-start.3 = ((f32[32,2,1536]{2,1,0:T(2,128)}), f32[32,2,1536]{2,1,0:T(2,128)}, u32[]{:S(2)}, u32[]{:S(2)}) async-start(f32[32,2,1536]{2,1,0:T(2,128)} %reshape.563), calls=%async_computation.5 | async-start | bytes 786432 | tf_op jit(solution)/shard_map/all_to_all | solution.py:46
  256.6 34.9 %collective-permute-start.2 = (bf16[1,3,32,1536]{3,2,1,0:T(8,128)(2,1)S(1)}, bf16[1,3,32,1536]{3,2,1,0:T(8,128)(2,1)S(1)}, u32[]{:S(2)}, u32[]{:S(2)}) collective-permute-start(bf16[1,3,32,1536]{3,2,1,0:T(8,128)(2,1)S(1)} %get-tuple-element.129), channel_id=1, source_target_pairs={{0,1},{1,2},{2,3},{4,5},{5,6},{6,7},{8,9},{9,10},{10,11},{12,13},{... | collective-permute-start | bytes 884744 | tf_op jit(solution)/shard_map/ppermute | solution.py:22
  258.7 33.5 %collective-permute-start.3 = (bf16[1,3,32,1536]{3,2,1,0:T(8,128)(2,1)S(1)}, bf16[1,3,32,1536]{3,2,1,0:T(8,128)(2,1)}, u32[]{:S(2)}, u32[]{:S(2)}) collective-permute-start(bf16[1,3,32,1536]{3,2,1,0:T(8,128)(2,1)S(1)} %get-tuple-element.130), channel_id=1, source_target_pairs={{1,0},{2,1},{3,2},{5,4},{6,5},{7,6},{9,8},{10,9},{11,10},{13,12},{... | collective-permute-start | bytes 884744 | tf_op jit(solution)/shard_map/ppermute | solution.py:23
  291.4 8.9 %copy-start.8 = (f32[1536]{0:T(1024)S(1)}, f32[1536]{0:T(1024)}, u32[]{:S(2)}) copy-start(f32[1536]{0:T(1024)} %copy-done.7) | copy-start | bytes 18436
  295.3 18.1 %all-to-all-start.4 = ((f32[32,2,1536]{2,1,0:T(2,128)}), f32[32,2,1536]{2,1,0:T(2,128)S(1)}, u32[]{:S(2)}, u32[]{:S(2)}) async-start(f32[32,2,1536]{2,1,0:T(2,128)} %broadcast_in_dim.11), calls=%async_computation.6 | async-start | bytes 786432 | tf_op jit(solution)/shard_map/all_to_all | solution.py:48
  315.2 5.8 %copy-start.1 = (bf16[1,4,32,1536]{3,2,1,0:T(8,128)(2,1)S(1)}, bf16[1,4,32,1536]{3,2,1,0:T(8,128)(2,1)}, u32[]{:S(2)}) copy-start(bf16[1,4,32,1536]{3,2,1,0:T(8,128)(2,1)} %param.7) | copy-start | bytes 1179652
  315.2 5.8 %copy-start.48 = (f32[1536]{0:T(1024)S(1)}, f32[1536]{0:T(1024)}, u32[]{:S(2)}) copy-start(f32[1536]{0:T(1024)} %param.12) | copy-start | bytes 18436
  317.4 19.4 %all-to-all-start.5 = ((bf16[2,384,768]{2,0,1:T(2,128)(2,1)}), bf16[2,384,768]{2,0,1:T(2,128)(2,1)S(1)}, u32[]{:S(2)}, u32[]{:S(2)}) async-start(bf16[2,384,768]{2,0,1:T(2,128)(2,1)} %copy.37), calls=%async_computation.7 | async-start | bytes 2359296 | tf_op jit(solution)/shard_map/all_to_all | solution.py:147
  (12 other events, 23.2 us)
Sparse Core Ops, SparseCore 0:
  30.9 67.5 all-gather.2
  100.6 53.6 all-gather.4
  172.4 60.5 reduce-scatter.2
  235.3 54.9 reduce-scatter.4
where the time goes:
time: 357 us; the launch traced here: 350 us
  waiting for transfers between devices  184 us (52%)
  other arithmetic  43 us (12%)
  starting transfers between devices  37.2 us (10%)
  matrix products  35.8 us (10%)
  local copies, waits for them, and re-layouts  34.4 us (10%)
  between operations  15.4 us (4%)
    all_to_all x1, waiting for transfers between devices, body(): up_loc = lax.all_to_all(pieces, ('dp', 'rows'), 0, 0, tiled=True)  44.8 us
    all_gather x1, waiting for transfers between devices, body(): down_loc = lax.all_gather(down_loc, 'dp', axis=1, tiled=True)  43.2 us
    reduce_scatter x1, waiting for transfers between devices, body(): lax.psum_scatter(jnp.stack([mlp_terms, norm_terms]).astype(jnp.bfloat16),...  42.1 us
    reduce_scatter x1, waiting for transfers between devices, body(): lax.psum_scatter(up_part.astype(jnp.bfloat16), 'dp', scatter_dimension=0,...  27.8 us
    all_to_all x1, waiting for transfers between devices, body(): lax.all_to_all(grad_sums, 'rows', 1, 2, tiled=True).astype(jnp.float32)  13.8 us
    reduce_sum x1, other arithmetic, body(): average = jnp.mean(flat, axis=-1, keepdims=True)  9.44 us
    convert_element_type x1, other arithmetic, body(): grad_x = (d_out.astype(jnp.float32) + back_conv).astype(jnp.bfloat16)  8.33 us
    dot_general x1, matrix products, body(): hidden = jnp.dot(gathered, up_loc, preferred_element_type=jnp.float32)  7.49 us
  transfers between devices with their start and end apart: 14, of which 7 were waited for; matrix products, arithmetic and copies ran while one was open for 20% of the time, Pallas kernels for 0%

commit v1 on v0

--- a/solution.py
+++ b/solution.py
@@ -63,7 +63,15 @@
     up_loc = lax.all_to_all(pieces, ("dp", "rows"), 0, 0, tiled=True)
     up_loc = up_loc.reshape(dp_size * row_size * block_c, sub)
     down_loc = lax.all_to_all(w_down, "rows", 0, 1, tiled=True)
-    down_loc = lax.all_gather(down_loc, "dp", axis=1, tiled=True)
+    count_2 = lax.axis_size("dp")
+    current, blocks = (down_loc, [down_loc])
+    for _ in range(count_2 - 1):
+        current = lax.ppermute(
+            current, "dp", [(i_2, (i_2 + 1) % count_2) for i_2 in range(count_2)]
+        )
+        blocks.insert(0, current)
+    merged = jnp.concatenate(blocks, axis=1)
+    down_loc = jnp.roll(merged, (lax.axis_index("dp") + 1) * down_loc.shape[1], axis=1)
     cotan = d_out.reshape(cells, width).astype(jnp.float32)
     back = (cotan * layer_scale).astype(jnp.bfloat16)
     rimmed = padded_2(feature_maps, (("rows", 1),), 3)

time: 357 us -> 368 us (1.031); the launches traced: 350 us -> 366 us
  starting transfers between devices: 37.2 us -> 51.4 us
  local copies, waits for them, and re-layouts: 34.4 us -> 46.2 us
  waiting for transfers between devices: 184 us -> 176 us
    ppermute x0 -> x3, waiting for transfers between devices: none -> 80.8 us  [body(): lax.ppermute(current, 'dp', [(i_2, (i_2 + 1) % count_2) for i_2 in range(...]
    all_to_all x1, waiting for transfers between devices: 44.8 us -> 0.01 us  [body(): up_loc = lax.all_to_all(pieces, ('dp', 'rows'), 0, 0, tiled=True)]
    all_gather x1 -> x0, waiting for transfers between devices: 43.2 us -> none  [body(): down_loc = lax.all_gather(down_loc, 'dp', axis=1, tiled=True)]
    ppermute x0 -> x3, starting transfers between devices: none -> 14.7 us  [body(): lax.ppermute(current, 'dp', [(i_2, (i_2 + 1) % count_2) for i_2 in range(...]
    unnamed x126 -> x135, local copies, waits for them, and re-layouts: 3.69 us -> 14.9 us
  transfers between devices with their start and end apart: 14 -> 16, of which waited for: 7 -> 8; matrix products, arithmetic and copies ran while one was open for 20% -> 20% of each run, Pallas kernels for 0% -> 0%
where the time goes in v1:
time: 368 us; the launch traced here: 366 us
  waiting for transfers between devices  176 us (48%)
  starting transfers between devices  51.4 us (14%)
  local copies, waits for them, and re-layouts  46.2 us (13%)
  other arithmetic  43 us (12%)
  matrix products  34.3 us (9%)
  between operations  15.2 us (4%)
    ppermute x3, waiting for transfers between devices, body(): lax.ppermute(current, 'dp', [(i_2, (i_2 + 1) % count_2) for i_2 in range(...  80.8 us
    reduce_scatter x1, waiting for transfers between devices, body(): lax.psum_scatter(jnp.stack([mlp_terms, norm_terms]).astype(jnp.bfloat16),...  42.7 us
    reduce_scatter x1, waiting for transfers between devices, body(): lax.psum_scatter(up_part.astype(jnp.bfloat16), 'dp', scatter_dimension=0,...  27.4 us
    unnamed x135, local copies, waits for them, and re-layouts  14.9 us
    ppermute x3, starting transfers between devices, body(): lax.ppermute(current, 'dp', [(i_2, (i_2 + 1) % count_2) for i_2 in range(...  14.7 us
    all_to_all x1, waiting for transfers between devices, body(): lax.all_to_all(grad_sums, 'rows', 1, 2, tiled=True).astype(jnp.float32)  13.6 us
    reduce_sum x1, other arithmetic, body(): average = jnp.mean(flat, axis=-1, keepdims=True)  9.44 us
    convert_element_type x1, other arithmetic, body(): grad_x = (d_out.astype(jnp.float32) + back_conv).astype(jnp.bfloat16)  8.33 us
  transfers between devices with their start and end apart: 16, of which 8 were waited for; matrix products, arithmetic and copies ran while one was open for 20% of the time, Pallas kernels for 0%

profile of v1, /device:TPU:0, one launch (start us, length us, event | category | flops | bytes accessed | tf_op | source)
XLA Modules:
  0.0 366.5 jit_solution(7568020447722689715)
XLA Ops:
  7.2 1.1 fusion.120
  8.3 2.4 collective-permute-start
  10.7 1.3 collective-permute-start.1
  12.0 1.4 slice_reduce_fusion.48
  13.5 1.8 slice_reduce_fusion.50
  15.6 2.4 slice_reduce_fusion.49
  18.1 1.1 maximum_convert_fusion
  19.2 9.4 %fusion.116 = (f32[4,32]{1,0:T(4,128)S(1)}, f32[1,4,32,1536]{3,2,1,0:T(8,128)S(1)}) fusion(f32[1536]{0:T(1024)S(1)} %get-tuple-element.119, f32[1536]{0:T(1024)S(1)} %get-tuple-element.120, f32[1536]{0:T(1024)S(1)} %get-tuple-element.73, f32[1536]{0:T(1024)S(1)} %get-tuple-element.74, f32[1,10,32,1536]{3,2,1,0:T(8,128)S(1)} %maximum_convert_fusion, ...), kind=kLoop, calls=%fused_computation.344 | loop fusion | flops 19267456 | bytes 8641024 | tf_op jit(solution)/shard_map/reduce_sum | solution.py:88
  29.8 0.9 pad_maximum_fusion.2
  31.9 6.1 %all-to-all-start.1 = ((bf16[4,768,96]{1,2,0:T(8,128)(2,1)}), bf16[4,768,96]{1,2,0:T(8,128)(2,1)S(1)}, u32[]{:S(2)}, u32[]{:S(2)}) async-start(bf16[4,768,96]{1,2,0:T(8,128)(2,1)} %bitcast.94), calls=%async_computation.1 | async-start | bytes 1179648 | tf_op jit(solution)/shard_map/all_to_all | solution.py:65
  38.1 2.5 reshape.558
  40.5 1.9 copy.34
  42.5 7.0 %all-to-all-done.1 = bf16[4,768,96]{1,2,0:T(8,128)(2,1)S(1)} async-done(((bf16[4,768,96]{1,2,0:T(8,128)(2,1)}), bf16[4,768,96]{1,2,0:T(8,128)(2,1)S(1)}, u32[]{:S(2)}, u32[]{:S(2)}) %all-to-all-start.1) | async-done | bytes 589856 | tf_op jit(solution)/shard_map/all_to_all | solution.py:65
  49.5 2.7 broadcast_in_dim.8
  52.2 5.3 %all-to-all-start = ((bf16[16,96,768]{2,1,0:T(8,128)(2,1)}), bf16[16,96,768]{2,1,0:T(8,128)(2,1)}, u32[]{:S(2)}, u32[]{:S(2)}) async-start(bf16[16,96,768]{2,1,0:T(8,128)(2,1)} %bitcast.84), calls=%async_computation | async-start | bytes 4718592 | tf_op jit(solution)/shard_map/all_to_all | solution.py:63
  57.5 1.9 collective-permute-start.2
  59.5 53.9 %collective-permute-done.2 = bf16[768,384]{0,1:T(8,128)(2,1)S(1)} collective-permute-done((bf16[768,384]{0,1:T(8,128)(2,1)S(1)}, bf16[768,384]{0,1:T(8,128)(2,1)S(1)}, u32[]{:S(2)}, u32[]{:S(2)}) %collective-permute-start.2) | collective-permute-done | bytes 589856 | tf_op jit(solution)/shard_map/ppermute | solution.py:69
  114.2 10.2 %collective-permute-start.3 = (bf16[768,384]{0,1:T(8,128)(2,1)S(1)}, bf16[768,384]{0,1:T(8,128)(2,1)}, u32[]{:S(2)}, u32[]{:S(2)}) collective-permute-start(bf16[768,384]{0,1:T(8,128)(2,1)S(1)} %collective-permute-done.2), channel_id=1, source_target_pairs={{0,8},{8,16},{16,24},{24,0},{1,9},{9,17},{17,25},{25,1},{2,10},{10... | collective-permute-start | bytes 1769480 | tf_op jit(solution)/shard_map/ppermute | solution.py:69
  124.4 12.4 %collective-permute-done.3 = bf16[768,384]{0,1:T(8,128)(2,1)} collective-permute-done((bf16[768,384]{0,1:T(8,128)(2,1)S(1)}, bf16[768,384]{0,1:T(8,128)(2,1)}, u32[]{:S(2)}, u32[]{:S(2)}) %collective-permute-start.3) | collective-permute-done | bytes 589856 | tf_op jit(solution)/shard_map/ppermute | solution.py:69
  136.8 2.6 collective-permute-start.4
  139.4 14.5 %collective-permute-done.4 = bf16[768,384]{0,1:T(8,128)(2,1)} collective-permute-done((bf16[768,384]{0,1:T(8,128)(2,1)}, bf16[768,384]{0,1:T(8,128)(2,1)}, u32[]{:S(2)}, u32[]{:S(2)}) %collective-permute-start.4) | collective-permute-done | bytes 589856 | tf_op jit(solution)/shard_map/ppermute | solution.py:69
  153.9 1.9 constant_dynamic-update-slice_fusion.7
  155.8 1.9 constant_dynamic-update-slice_fusion.6
  158.6 0.9 constant_dynamic-update-slice_fusion.4
  159.5 2.0 constant_dynamic-update-slice_fusion.3
  161.4 1.9 constant_dynamic-update-slice_fusion.2
  165.1 5.1 %multiply_convert_fusion = (bf16[1024,768]{1,0:T(8,128)(2,1)S(1)}, f32[1024,768]{1,0:T(8,128)S(1)}) fusion(bf16[1536,768]{1,0:T(8,128)(2,1)} %bitcast.5, bf16[2,1024,1536]{2,1,0:T(8,128)(2,1)} %all-gather.2.cloned.1.call-done), kind=kOutput, calls=%fused_computation.100 | convolution fusion | flops 2419851264 | bytes 10223616 | tf_op jit(solution)/shard_map/dot_general | solution.py:96
  170.2 5.2 %fusion = bf16[1,1024,1536]{2,1,0:T(8,128)(2,1)S(1)} fusion(bf16[1024,768]{1,0:T(8,128)(2,1)S(1)} %get-tuple-element.133, bf16[768,3072]{0,1:T(8,128)(2,1)} %constant_dynamic-update-slice_fusion, s32[]{:T(128)S(6)} %select_n.14), kind=kOutput, calls=%fused_computation.90 | convolution fusion | flops 2417491968 | bytes 7077892 | tf_op jit(solution)/shard_map/dot_general | solution.py:98
  175.5 5.2 %fusion.7 = bf16[1024,768]{1,0:T(8,128)(2,1)S(1)} fusion(f32[1024,768]{1,0:T(8,128)S(1)} %get-tuple-element.134, bf16[768,3072]{0,1:T(8,128)(2,1)} %constant_dynamic-update-slice_fusion, s32[]{:T(128)S(6)} %select_n.14, bf16[2,1024,1536]{2,1,0:T(8,128)(2,1)S(1)} %copy-done.60), kind=kOutput, calls=%fused_computation.97 | convolution fusion | flops 2423783424 | bytes 10223620 | tf_op jit(solution)/shard_map/dot_general | solution.py:102
  180.7 5.1 %fusion.1 = bf16[1,1024,1536]{2,1,0:T(8,128)(2,1)S(1)} fusion(bf16[1024,768]{1,0:T(8,128)(2,1)S(1)} %fusion.7, bf16[1536,768]{1,0:T(8,128)(2,1)} %bitcast.5), kind=kOutput, calls=%fused_computation.91 | convolution fusion | flops 2417491968 | bytes 7077888 | tf_op jit(solution)/shard_map/dot_general | solution.py:109
  185.9 3.2 pad_maximum_fusion
  189.1 6.5 %convolution_convert_fusion.3 = bf16[1536,768]{1,0:T(8,128)(2,1)} fusion(bf16[1024,768]{1,0:T(8,128)(2,1)} %copy-done.62, bf16[2,1024,1536]{2,1,0:T(8,128)(2,1)} %all-gather.2.cloned.1.call-done), kind=kOutput, calls=%fused_computation.89 | convolution fusion | flops 2417098752 | bytes 7077888 | tf_op jit(solution)/shard_map/dot_general | solution.py:106
  195.6 7.2 %convolution_convert_fusion.2 = bf16[1536,768]{1,0:T(8,128)(2,1)} fusion(bf16[1024,768]{1,0:T(8,128)(2,1)} %copy-done.61, bf16[2,1024,1536]{2,1,0:T(8,128)(2,1)} %all-gather.2.cloned.1.call-done), kind=kOutput, calls=%fused_computation.88 | convolution fusion | flops 2417098752 | bytes 7077888 | tf_op jit(solution)/shard_map/dot_general | solution.py:99
  202.8 4.7 %all-to-all-start.2 = ((bf16[4,384,768]{2,1,0:T(8,128)(2,1)}), bf16[4,384,768]{2,1,0:T(8,128)(2,1)}, u32[]{:S(2)}, u32[]{:S(2)}) async-start(bf16[4,384,768]{2,1,0:T(8,128)(2,1)} %bitcast.93), calls=%async_computation.4 | async-start | bytes 4718592 | tf_op jit(solution)/shard_map/all_to_all | solution.py:123
  207.5 42.7 %reduce-scatter.3.cloned.1.call-done = bf16[2,128,1536]{2,1,0:T(8,128)(2,1)} async-done(((bf16[2,1024,1536]{2,1,0:T(8,128)(2,1)}), bf16[2,128,1536]{2,1,0:T(8,128)(2,1)}) %reduce-scatter.3.cloned.1.call-update) | async-done | bytes 786448 | tf_op jit(solution)/shard_map/reduce_scatter | solution.py:112
  250.2 1.4 convert_element_type.120
  251.6 2.1 fusion.108
  254.8 1.3 div.22
  256.1 1.2 broadcast_multiply_fusion.1
  257.3 1.3 div.24
  258.6 1.3 broadcast_in_dim.10
  259.9 1.0 fusion.118
  260.9 2.4 multiply_reduce_fusion
  263.5 2.0 multiply_reduce_fusion.18
  265.6 1.4 multiply_reduce_fusion.36
  268.0 1.0 reshape.563
  269.0 4.7 %all-to-all-start.3 = ((f32[32,2,1536]{2,1,0:T(2,128)}), f32[32,2,1536]{2,1,0:T(2,128)}, u32[]{:S(2)}, u32[]{:S(2)}) async-start(f32[32,2,1536]{2,1,0:T(2,128)} %reshape.563), calls=%async_computation.5 | async-start | bytes 786432 | tf_op jit(solution)/shard_map/all_to_all | solution.py:46
  273.8 2.1 collective-permute-start.5
  275.9 1.3 collective-permute-start.6
  277.2 2.3 reduce_sum.518
  279.5 27.4 %reduce-scatter.5.cloned.1.call-done = bf16[384,768]{1,0:T(8,128)(2,1)} async-done(((bf16[1536,768]{1,0:T(8,128)(2,1)}), bf16[384,768]{1,0:T(8,128)(2,1)}) %reduce-scatter.5.cloned.1.call-update) | async-done | bytes 589840 | tf_op jit(solution)/shard_map/reduce_scatter | solution.py:124
  306.9 1.2 pad_maximum_fusion.1
  308.8 1.2 maximum_convert_fusion.1
  310.0 1.1 reduce_sum.572
  312.0 4.9 %all-to-all-start.4 = ((f32[32,2,1536]{2,1,0:T(2,128)}), f32[32,2,1536]{2,1,0:T(2,128)S(1)}, u32[]{:S(2)}, u32[]{:S(2)}) async-start(f32[32,2,1536]{2,1,0:T(2,128)} %broadcast_in_dim.11), calls=%async_computation.6 | async-start | bytes 786432 | tf_op jit(solution)/shard_map/all_to_all | solution.py:48
  316.9 8.3 %fusion.101 = bf16[1,4,32,1536]{3,2,1,0:T(8,128)(2,1)} fusion(f32[1,10,32,1536]{3,2,1,0:T(8,128)S(1)} %maximum_convert_fusion.1, f32[1536]{0:T(1024)} %copy-done.17, f32[1536]{0:T(1024)} %copy-done.18, f32[1536]{0:T(1024)} %copy-done.20, f32[1536]{0:T(1024)} %copy-done.21, f32[1536]{0:T(1024)} %copy-done.22, f32[1536]{0:T(1024)} %copy-done.23, ...), kind=kLoop, calls=%fused_computation.197 | loop fusion | flops 19660800 | bytes 8562688 | tf_op jit(solution)/shard_map/convert_element_type | solution.py:150
  325.2 4.8 %all-to-all-done.4 = f32[32,2,1536]{2,1,0:T(2,128)S(1)} async-done(((f32[32,2,1536]{2,1,0:T(2,128)}), f32[32,2,1536]{2,1,0:T(2,128)S(1)}, u32[]{:S(2)}, u32[]{:S(2)}) %all-to-all-start.4) | async-done | bytes 393248 | tf_op jit(solution)/shard_map/all_to_all | solution.py:48
  331.7 2.2 copy.37
  334.0 3.8 %all-to-all-start.5 = ((bf16[2,384,768]{2,0,1:T(2,128)(2,1)}), bf16[2,384,768]{2,0,1:T(2,128)(2,1)S(1)}, u32[]{:S(2)}, u32[]{:S(2)}) async-start(bf16[2,384,768]{2,0,1:T(2,128)(2,1)} %copy.37), calls=%async_computation.7 | async-start | bytes 2359296 | tf_op jit(solution)/shard_map/all_to_all | solution.py:155
  337.8 2.0 add_convert_fusion
  339.8 13.6 %all-to-all-done.5 = bf16[2,384,768]{2,0,1:T(2,128)(2,1)S(1)} async-done(((bf16[2,384,768]{2,0,1:T(2,128)(2,1)}), bf16[2,384,768]{2,0,1:T(2,128)(2,1)S(1)}, u32[]{:S(2)}, u32[]{:S(2)}) %all-to-all-start.5) | async-done | bytes 1179680 | tf_op jit(solution)/shard_map/all_to_all | solution.py:155
  354.1 1.8 fusion.117
  356.7 1.2 copy.43
  358.7 1.2 copy.42
  (212 shorter events, 13.2 us)
Async XLA Ops:
  7.2 158.0 %all-gather.2.cloned.1.call-start = ((), (), s32[]{:S(2)}) async-start(), calls=%async_computation.8 | async-start | bytes 7077888 | tf_op jit(solution)/shard_map/all_gather | solution.py:94
  8.3 9.7 %collective-permute-start = (bf16[1,3,32,1536]{3,2,1,0:T(8,128)(2,1)S(1)}, bf16[1,3,32,1536]{3,2,1,0:T(8,128)(2,1)S(1)}, u32[]{:S(2)}, u32[]{:S(2)}) collective-permute-start(bf16[1,3,32,1536]{3,2,1,0:T(8,128)(2,1)S(1)} %get-tuple-element.131), channel_id=1, source_target_pairs={{0,1},{1,2},{2,3},{4,5},{5,6},{6,7},{8,9},{9,10},{10,11},{12,13},{... | collective-permute-start | bytes 884744 | tf_op jit(solution)/shard_map/ppermute | solution.py:22
  10.7 7.3 %collective-permute-start.1 = (bf16[1,3,32,1536]{3,2,1,0:T(8,128)(2,1)S(1)}, bf16[1,3,32,1536]{3,2,1,0:T(8,128)(2,1)S(1)}, u32[]{:S(2)}, u32[]{:S(2)}) collective-permute-start(bf16[1,3,32,1536]{3,2,1,0:T(8,128)(2,1)S(1)} %get-tuple-element.132), channel_id=1, source_target_pairs={{1,0},{2,1},{3,2},{5,4},{6,5},{7,6},{9,8},{10,9},{11,10},{13,12},{... | collective-permute-start | bytes 884744 | tf_op jit(solution)/shard_map/ppermute | solution.py:23
  13.4 15.3 %copy-start.8 = (f32[1536]{0:T(1024)}, f32[1536]{0:T(1024)S(1)}, u32[]{:S(2)}) copy-start(f32[1536]{0:T(1024)S(1)} %get-tuple-element.111) | copy-start | bytes 18436
  13.4 15.3 %copy-start.10 = (f32[1536]{0:T(1024)}, f32[1536]{0:T(1024)S(1)}, u32[]{:S(2)}) copy-start(f32[1536]{0:T(1024)S(1)} %get-tuple-element.112) | copy-start | bytes 18436
  13.4 15.3 %copy-start.11 = (f32[1536]{0:T(1024)}, f32[1536]{0:T(1024)S(1)}, u32[]{:S(2)}) copy-start(f32[1536]{0:T(1024)S(1)} %get-tuple-element.113) | copy-start | bytes 18436
  13.4 15.3 %copy-start.12 = (f32[1536]{0:T(1024)}, f32[1536]{0:T(1024)S(1)}, u32[]{:S(2)}) copy-start(f32[1536]{0:T(1024)S(1)} %get-tuple-element.114) | copy-start | bytes 18436
  13.5 15.3 %copy-start.13 = (f32[1536]{0:T(1024)}, f32[1536]{0:T(1024)S(1)}, u32[]{:S(2)}) copy-start(f32[1536]{0:T(1024)S(1)} %get-tuple-element.115) | copy-start | bytes 18436
  13.5 15.3 %copy-start.14 = (f32[1536]{0:T(1024)}, f32[1536]{0:T(1024)S(1)}, u32[]{:S(2)}) copy-start(f32[1536]{0:T(1024)S(1)} %get-tuple-element.116) | copy-start | bytes 18436
  13.5 15.3 %copy-start.15 = (f32[1536]{0:T(1024)}, f32[1536]{0:T(1024)S(1)}, u32[]{:S(2)}) copy-start(f32[1536]{0:T(1024)S(1)} %get-tuple-element.117) | copy-start | bytes 18436
  13.5 15.3 %copy-start.16 = (f32[1536]{0:T(1024)}, f32[1536]{0:T(1024)S(1)}, u32[]{:S(2)}) copy-start(f32[1536]{0:T(1024)S(1)} %get-tuple-element.118) | copy-start | bytes 18436
  13.5 15.3 %copy-start.17 = (f32[1536]{0:T(1024)}, f32[1536]{0:T(1024)S(1)}, u32[]{:S(2)}) copy-start(f32[1536]{0:T(1024)S(1)} %get-tuple-element.119) | copy-start | bytes 18436
  13.5 15.3 %copy-start.18 = (f32[1536]{0:T(1024)}, f32[1536]{0:T(1024)S(1)}, u32[]{:S(2)}) copy-start(f32[1536]{0:T(1024)S(1)} %get-tuple-element.120) | copy-start | bytes 18436
  15.4 13.4 %copy-start.19 = (f32[1536]{0:T(1024)}, f32[1536]{0:T(1024)S(1)}, u32[]{:S(2)}) copy-start(f32[1536]{0:T(1024)S(1)} %get-tuple-element.72) | copy-start | bytes 18436
  15.4 13.4 %copy-start.20 = (f32[1536]{0:T(1024)}, f32[1536]{0:T(1024)S(1)}, u32[]{:S(2)}) copy-start(f32[1536]{0:T(1024)S(1)} %get-tuple-element.73) | copy-start | bytes 18436
  15.4 13.4 %copy-start.21 = (f32[1536]{0:T(1024)}, f32[1536]{0:T(1024)S(1)}, u32[]{:S(2)}) copy-start(f32[1536]{0:T(1024)S(1)} %get-tuple-element.74) | copy-start | bytes 18436
  15.4 13.4 %copy-start.22 = (f32[1536]{0:T(1024)}, f32[1536]{0:T(1024)S(1)}, u32[]{:S(2)}) copy-start(f32[1536]{0:T(1024)S(1)} %get-tuple-element.75) | copy-start | bytes 18436
  15.4 13.4 %copy-start.23 = (f32[1536]{0:T(1024)}, f32[1536]{0:T(1024)S(1)}, u32[]{:S(2)}) copy-start(f32[1536]{0:T(1024)S(1)} %get-tuple-element.76) | copy-start | bytes 18436
  15.4 13.4 %copy-start.24 = (f32[1536]{0:T(1024)}, f32[1536]{0:T(1024)S(1)}, u32[]{:S(2)}) copy-start(f32[1536]{0:T(1024)S(1)} %get-tuple-element.77) | copy-start | bytes 18436
  15.4 13.4 %copy-start.25 = (f32[1536]{0:T(1024)}, f32[1536]{0:T(1024)S(1)}, u32[]{:S(2)}) copy-start(f32[1536]{0:T(1024)S(1)} %get-tuple-element.78) | copy-start | bytes 18436
  15.4 13.4 %copy-start.26 = (f32[1536]{0:T(1024)}, f32[1536]{0:T(1024)S(1)}, u32[]{:S(2)}) copy-start(f32[1536]{0:T(1024)S(1)} %get-tuple-element.79) | copy-start | bytes 18436
  15.4 13.4 %copy-start.27 = (f32[1536]{0:T(1024)}, f32[1536]{0:T(1024)S(1)}, u32[]{:S(2)}) copy-start(f32[1536]{0:T(1024)S(1)} %get-tuple-element.80) | copy-start | bytes 18436
  15.5 13.4 %copy-start.28 = (f32[1536]{0:T(1024)}, f32[1536]{0:T(1024)S(1)}, u32[]{:S(2)}) copy-start(f32[1536]{0:T(1024)S(1)} %get-tuple-element.81) | copy-start | bytes 18436
  15.5 13.4 %copy-start.29 = (f32[1536]{0:T(1024)}, f32[1536]{0:T(1024)S(1)}, u32[]{:S(2)}) copy-start(f32[1536]{0:T(1024)S(1)} %get-tuple-element.82) | copy-start | bytes 18436
  15.5 13.4 %copy-start.30 = (f32[1536]{0:T(1024)}, f32[1536]{0:T(1024)S(1)}, u32[]{:S(2)}) copy-start(f32[1536]{0:T(1024)S(1)} %get-tuple-element.83) | copy-start | bytes 18436
  15.5 13.4 %copy-start.31 = (f32[1536]{0:T(1024)}, f32[1536]{0:T(1024)S(1)}, u32[]{:S(2)}) copy-start(f32[1536]{0:T(1024)S(1)} %get-tuple-element.84) | copy-start | bytes 18436
  15.5 13.4 %copy-start.32 = (f32[1536]{0:T(1024)}, f32[1536]{0:T(1024)S(1)}, u32[]{:S(2)}) copy-start(f32[1536]{0:T(1024)S(1)} %get-tuple-element.85) | copy-start | bytes 18436
  15.5 13.4 %copy-start.33 = (f32[1536]{0:T(1024)}, f32[1536]{0:T(1024)S(1)}, u32[]{:S(2)}) copy-start(f32[1536]{0:T(1024)S(1)} %get-tuple-element.86) | copy-start | bytes 18436
  15.5 13.4 %copy-start.34 = (f32[1536]{0:T(1024)}, f32[1536]{0:T(1024)S(1)}, u32[]{:S(2)}) copy-start(f32[1536]{0:T(1024)S(1)} %get-tuple-element.87) | copy-start | bytes 18436
  15.5 13.4 %copy-start.35 = (f32[1536]{0:T(1024)}, f32[1536]{0:T(1024)S(1)}, u32[]{:S(2)}) copy-start(f32[1536]{0:T(1024)S(1)} %get-tuple-element.88) | copy-start | bytes 18436
  15.5 13.4 %copy-start.36 = (f32[1536]{0:T(1024)}, f32[1536]{0:T(1024)S(1)}, u32[]{:S(2)}) copy-start(f32[1536]{0:T(1024)S(1)} %get-tuple-element.89) | copy-start | bytes 18436
  15.5 13.4 %copy-start.37 = (f32[1536]{0:T(1024)}, f32[1536]{0:T(1024)S(1)}, u32[]{:S(2)}) copy-start(f32[1536]{0:T(1024)S(1)} %get-tuple-element.90) | copy-start | bytes 18436
  18.0 11.0 %copy-start.38 = (f32[1536]{0:T(1024)}, f32[1536]{0:T(1024)S(1)}, u32[]{:S(2)}) copy-start(f32[1536]{0:T(1024)S(1)} %get-tuple-element.91) | copy-start | bytes 18436
  18.0 11.0 %copy-start.39 = (f32[1536]{0:T(1024)}, f32[1536]{0:T(1024)S(1)}, u32[]{:S(2)}) copy-start(f32[1536]{0:T(1024)S(1)} %get-tuple-element.92) | copy-start | bytes 18436
  18.0 11.0 %copy-start.40 = (f32[1536]{0:T(1024)}, f32[1536]{0:T(1024)S(1)}, u32[]{:S(2)}) copy-start(f32[1536]{0:T(1024)S(1)} %get-tuple-element.93) | copy-start | bytes 18436
  18.0 11.0 %copy-start.41 = (f32[1536]{0:T(1024)}, f32[1536]{0:T(1024)S(1)}, u32[]{:S(2)}) copy-start(f32[1536]{0:T(1024)S(1)} %get-tuple-element.94) | copy-start | bytes 18436
  18.0 11.0 %copy-start.42 = (f32[1536]{0:T(1024)}, f32[1536]{0:T(1024)S(1)}, u32[]{:S(2)}) copy-start(f32[1536]{0:T(1024)S(1)} %get-tuple-element.95) | copy-start | bytes 18436
  18.0 11.0 %copy-start.43 = (f32[1536]{0:T(1024)}, f32[1536]{0:T(1024)S(1)}, u32[]{:S(2)}) copy-start(f32[1536]{0:T(1024)S(1)} %get-tuple-element.96) | copy-start | bytes 18436
  18.0 11.0 %copy-start.44 = (f32[1536]{0:T(1024)}, f32[1536]{0:T(1024)S(1)}, u32[]{:S(2)}) copy-start(f32[1536]{0:T(1024)S(1)} %get-tuple-element.97) | copy-start | bytes 18436
  18.0 11.0 %copy-start.45 = (f32[1536]{0:T(1024)}, f32[1536]{0:T(1024)S(1)}, u32[]{:S(2)}) copy-start(f32[1536]{0:T(1024)S(1)} %get-tuple-element.98) | copy-start | bytes 18436
  18.0 11.0 %copy-start.46 = (f32[1536]{0:T(1024)}, f32[1536]{0:T(1024)S(1)}, u32[]{:S(2)}) copy-start(f32[1536]{0:T(1024)S(1)} %get-tuple-element.99) | copy-start | bytes 18436
  18.0 11.0 %copy-start.47 = (f32[1536]{0:T(1024)}, f32[1536]{0:T(1024)S(1)}, u32[]{:S(2)}) copy-start(f32[1536]{0:T(1024)S(1)} %get-tuple-element.100) | copy-start | bytes 18436
  19.2 10.3 %copy-start.2 = (bf16[1,4,32,1536]{3,2,1,0:T(8,128)(2,1)S(1)}, bf16[1,4,32,1536]{3,2,1,0:T(8,128)(2,1)}, u32[]{:S(2)}) copy-start(bf16[1,4,32,1536]{3,2,1,0:T(8,128)(2,1)} %param.13) | copy-start | bytes 1179652
  19.2 10.3 %copy-start.7 = (f32[1536]{0:T(1024)S(1)}, f32[1536]{0:T(1024)}, u32[]{:S(2)}) copy-start(f32[1536]{0:T(1024)} %param.9) | copy-start | bytes 18436
  19.2 10.3 %copy-start.48 = (f32[1536]{0:T(1024)S(1)}, f32[1536]{0:T(1024)}, u32[]{:S(2)}) copy-start(f32[1536]{0:T(1024)} %param.12) | copy-start | bytes 18436
  31.9 17.6 %all-to-all-start.1 = ((bf16[4,768,96]{1,2,0:T(8,128)(2,1)}), bf16[4,768,96]{1,2,0:T(8,128)(2,1)S(1)}, u32[]{:S(2)}, u32[]{:S(2)}) async-start(bf16[4,768,96]{1,2,0:T(8,128)(2,1)} %bitcast.94), calls=%async_computation.1 | async-start | bytes 1179648 | tf_op jit(solution)/shard_map/all_to_all | solution.py:65
  52.2 112.9 %all-to-all-start = ((bf16[16,96,768]{2,1,0:T(8,128)(2,1)}), bf16[16,96,768]{2,1,0:T(8,128)(2,1)}, u32[]{:S(2)}, u32[]{:S(2)}) async-start(bf16[16,96,768]{2,1,0:T(8,128)(2,1)} %bitcast.84), calls=%async_computation | async-start | bytes 4718592 | tf_op jit(solution)/shard_map/all_to_all | solution.py:63
  57.5 192.7 %reduce-scatter.3.cloned.1.call-start = ((), (), s32[]{:S(2)}) async-start(), calls=%async_computation.9 | async-start | bytes 7077888 | tf_op jit(solution)/shard_map/reduce_scatter | solution.py:112
  57.5 55.9 %collective-permute-start.2 = (bf16[768,384]{0,1:T(8,128)(2,1)S(1)}, bf16[768,384]{0,1:T(8,128)(2,1)S(1)}, u32[]{:S(2)}, u32[]{:S(2)}) collective-permute-start(bf16[768,384]{0,1:T(8,128)(2,1)S(1)} %bitcast.85), channel_id=1, source_target_pairs={{0,8},{8,16},{16,24},{24,0},{1,9},{9,17},{17,25},{25,1},{2,10},{10... | collective-permute-start | bytes 1769480 | tf_op jit(solution)/shard_map/ppermute | solution.py:69
  114.2 22.6 %collective-permute-start.3 = (bf16[768,384]{0,1:T(8,128)(2,1)S(1)}, bf16[768,384]{0,1:T(8,128)(2,1)}, u32[]{:S(2)}, u32[]{:S(2)}) collective-permute-start(bf16[768,384]{0,1:T(8,128)(2,1)S(1)} %collective-permute-done.2), channel_id=1, source_target_pairs={{0,8},{8,16},{16,24},{24,0},{1,9},{9,17},{17,25},{25,1},{2,10},{10... | collective-permute-start | bytes 1769480 | tf_op jit(solution)/shard_map/ppermute | solution.py:69
  136.8 17.1 %collective-permute-start.4 = (bf16[768,384]{0,1:T(8,128)(2,1)}, bf16[768,384]{0,1:T(8,128)(2,1)}, u32[]{:S(2)}, u32[]{:S(2)}) collective-permute-start(bf16[768,384]{0,1:T(8,128)(2,1)} %collective-permute-done.3), channel_id=1, source_target_pairs={{0,8},{8,16},{16,24},{24,0},{1,9},{9,17},{17,25},{25,1},{2,10},{10... | collective-permute-start | bytes 1769480 | tf_op jit(solution)/shard_map/ppermute | solution.py:69
  139.4 18.3 %copy-start.4 = (bf16[768,384]{0,1:T(8,128)(2,1)S(1)}, bf16[768,384]{0,1:T(8,128)(2,1)}, u32[]{:S(2)}) copy-start(bf16[768,384]{0,1:T(8,128)(2,1)} %copy-done.3) | copy-start | bytes 1769476
  170.2 5.2 %copy-start.61 = (bf16[1024,768]{1,0:T(8,128)(2,1)}, bf16[1024,768]{1,0:T(8,128)(2,1)S(1)}, u32[]{:S(2)}) copy-start(bf16[1024,768]{1,0:T(8,128)(2,1)S(1)} %get-tuple-element.133) | copy-start | bytes 4718596
  189.1 117.8 %reduce-scatter.5.cloned.1.call-start = ((), (), s32[]{:S(2)}) async-start(), calls=%async_computation.10 | async-start | bytes 2949120 | tf_op jit(solution)/shard_map/reduce_scatter | solution.py:124
  202.8 66.2 %all-to-all-start.2 = ((bf16[4,384,768]{2,1,0:T(8,128)(2,1)}), bf16[4,384,768]{2,1,0:T(8,128)(2,1)}, u32[]{:S(2)}, u32[]{:S(2)}) async-start(bf16[4,384,768]{2,1,0:T(8,128)(2,1)} %bitcast.93), calls=%async_computation.4 | async-start | bytes 4718592 | tf_op jit(solution)/shard_map/all_to_all | solution.py:123
  250.2 9.7 %copy-start = (bf16[2,128,1536]{2,1,0:T(8,128)(2,1)S(1)}, bf16[2,128,1536]{2,1,0:T(8,128)(2,1)}, u32[]{:S(2)}) copy-start(bf16[2,128,1536]{2,1,0:T(8,128)(2,1)} %reduce-scatter.3.cloned.1.call-done) | copy-start | bytes 2359300
  269.0 41.0 %all-to-all-start.3 = ((f32[32,2,1536]{2,1,0:T(2,128)}), f32[32,2,1536]{2,1,0:T(2,128)}, u32[]{:S(2)}, u32[]{:S(2)}) async-start(f32[32,2,1536]{2,1,0:T(2,128)} %reshape.563), calls=%async_computation.5 | async-start | bytes 786432 | tf_op jit(solution)/shard_map/all_to_all | solution.py:46
  273.8 34.3 %collective-permute-start.5 = (bf16[1,3,32,1536]{3,2,1,0:T(8,128)(2,1)S(1)}, bf16[1,3,32,1536]{3,2,1,0:T(8,128)(2,1)S(1)}, u32[]{:S(2)}, u32[]{:S(2)}) collective-permute-start(bf16[1,3,32,1536]{3,2,1,0:T(8,128)(2,1)S(1)} %get-tuple-element.129), channel_id=1, source_target_pairs={{0,1},{1,2},{2,3},{4,5},{5,6},{6,7},{8,9},{9,10},{10,11},{12,13},{... | collective-permute-start | bytes 884744 | tf_op jit(solution)/shard_map/ppermute | solution.py:22
  275.9 32.9 %collective-permute-start.6 = (bf16[1,3,32,1536]{3,2,1,0:T(8,128)(2,1)S(1)}, bf16[1,3,32,1536]{3,2,1,0:T(8,128)(2,1)}, u32[]{:S(2)}, u32[]{:S(2)}) collective-permute-start(bf16[1,3,32,1536]{3,2,1,0:T(8,128)(2,1)S(1)} %get-tuple-element.130), channel_id=1, source_target_pairs={{1,0},{2,1},{3,2},{5,4},{6,5},{7,6},{9,8},{10,9},{11,10},{13,12},{... | collective-permute-start | bytes 884744 | tf_op jit(solution)/shard_map/ppermute | solution.py:23
  308.0 8.8 %copy-start.9 = (f32[1536]{0:T(1024)S(1)}, f32[1536]{0:T(1024)}, u32[]{:S(2)}) copy-start(f32[1536]{0:T(1024)} %copy-done.8) | copy-start | bytes 18436
  312.0 18.1 %all-to-all-start.4 = ((f32[32,2,1536]{2,1,0:T(2,128)}), f32[32,2,1536]{2,1,0:T(2,128)S(1)}, u32[]{:S(2)}, u32[]{:S(2)}) async-start(f32[32,2,1536]{2,1,0:T(2,128)} %broadcast_in_dim.11), calls=%async_computation.6 | async-start | bytes 786432 | tf_op jit(solution)/shard_map/all_to_all | solution.py:48
  331.7 6.0 %copy-start.1 = (bf16[1,4,32,1536]{3,2,1,0:T(8,128)(2,1)S(1)}, bf16[1,4,32,1536]{3,2,1,0:T(8,128)(2,1)}, u32[]{:S(2)}) copy-start(bf16[1,4,32,1536]{3,2,1,0:T(8,128)(2,1)} %param.7) | copy-start | bytes 1179652
  331.7 6.0 %copy-start.49 = (f32[1536]{0:T(1024)S(1)}, f32[1536]{0:T(1024)}, u32[]{:S(2)}) copy-start(f32[1536]{0:T(1024)} %param.12) | copy-start | bytes 18436
  334.0 19.4 %all-to-all-start.5 = ((bf16[2,384,768]{2,0,1:T(2,128)(2,1)}), bf16[2,384,768]{2,0,1:T(2,128)(2,1)S(1)}, u32[]{:S(2)}, u32[]{:S(2)}) async-start(bf16[2,384,768]{2,0,1:T(2,128)(2,1)} %copy.37), calls=%async_computation.7 | async-start | bytes 2359296 | tf_op jit(solution)/shard_map/all_to_all | solution.py:155
  (15 other events, 34.4 us)
Sparse Core Ops, SparseCore 0:
  30.9 67.3 all-gather.1
  189.2 60.9 reduce-scatter.2
  252.6 54.2 reduce-scatter.4
